TPU v7x, 256 devices: a whole 4x4x8 slice. The times are simulated.
256 devices in a mesh: blk: 32 (over x, y, core), sub: 8 (over z).
Axes of the slice: x: 4, y: 4, z: 8, core: 2. Of those that a mesh axis runs over, the one named last changes fastest.
Arguments:
- block_vec: bfloat16 [64, 512, 512], P('blk', 'sub'), may hold values from -6 to 6
- left_factor: bfloat16 [8, 512, 512], replicated, may hold values from -0.25 to 0.25
- right_factor: bfloat16 [8, 512, 512], replicated, may hold values from -0.25 to 0.25
- pairs: int32 [32, 32, 2, 3], replicated, may hold values from 0 to 7, as said below
- pair_count: int32 [32, 32], replicated, may hold values from 1 to 2, as said below
- left_basis: bfloat16 [64, 512, 512], P('blk'), may hold values from -0.25 to 0.25
- left_dual: bfloat16 [64, 512, 512], P('blk'), may hold values from -0.25 to 0.25
- right_eigenvector_matrix: bfloat16 [64, 512, 512], P('blk'), may hold values from -0.25 to 0.25
- right_dual: bfloat16 [64, 512, 512], P('blk'), may hold values from -0.25 to 0.25
- left_rates: float32 [64, 512], P('blk', 'sub'), may hold values from 0.5 to 8
- right_rates: float32 [64, 512], P('blk'), may hold values from 0.5 to 8
Outputs:
- next_vec: float32 [64, 512, 512], P('blk', None, 'sub')
Inputs may be any that keep to these rules, and one draw needn't show every extreme that they name: `pairs`: entry [g, h, c, 0] is a source block index within group g, [g, h, c, 1] a target block index within group h (0 to 1), and [g, h, c, 2] a term index (0 to 7); where g equals h, source and target differ. For some target group h, pair_count[g, h] is 2 for every g.
All inputs are finite; a program needn't handle non-finite values.
Results may differ from a plain program's by a relative error of at most 0.023.
Values may be sent and summed in bfloat16 or wider, within the bound.
No kernel may reach another device: no remote copies, remote signals or barrier semaphores. Data moves between devices by JAX's collectives and lax.ppermute only.
A program may use at most 64 MiB of HBM per device.

v0:
```python
import jax
import jax.numpy as jnp
from jax import lax
from jax.sharding import PartitionSpec as P


def local(
    block_vec,
    left_factor,
    right_factor,
    pairs,
    pair_count,
    left_basis,
    left_dual,
    right_eigenvector_matrix,
    right_dual,
    left_rates,
    right_rates,
):
    owner = lax.axis_index("blk")
    groups = lax.axis_size("blk")
    local_blocks = block_vec.shape[0]
    row_count = block_vec.shape[1]
    width_two = block_vec.shape[2]
    slots_per = pairs.shape[2]
    term_total = left_factor.shape[0]
    all_count = groups * local_blocks
    incoming = lax.dynamic_index_in_dim(pairs, owner, 1, keepdims=False)
    counts = lax.dynamic_index_in_dim(pair_count, owner, 1, keepdims=False)
    live_mask = (jnp.arange(slots_per)[None, :] < counts[:, None]).astype(jnp.float32)
    target_term = incoming[..., 1] * term_total + incoming[..., 2]
    source = jnp.arange(groups, dtype=jnp.int32)[:, None] * local_blocks + incoming[..., 0]
    key_onehot = (
        target_term[..., None] == jnp.arange(local_blocks * term_total)[None, None, :]
    ).astype(jnp.float32) * live_mask[..., None]
    source_onehot = (source[..., None] == jnp.arange(all_count)[None, None, :]).astype(jnp.float32)
    weights = jnp.einsum("gqk,gqs->ks", key_onehot, source_onehot).astype(jnp.bfloat16)
    everything = lax.all_gather(block_vec, "blk", axis=0, tiled=True)
    pooled = jnp.einsum(
        "ks,srn->krn", weights, everything, preferred_element_type=jnp.float32
    ).astype(jnp.bfloat16)
    pooled = pooled.reshape(local_blocks, term_total, row_count, width_two)
    right_done = jnp.einsum(
        "ktrn,tmn->ktrm", pooled, right_factor, preferred_element_type=jnp.float32
    ).astype(jnp.bfloat16)
    right_cols = lax.all_to_all(right_done, "sub", split_axis=3, concat_axis=2, tiled=True)
    summed = jnp.einsum(
        "tab,ktbc->kac", left_factor, right_cols, preferred_element_type=jnp.float32
    ).astype(jnp.bfloat16)
    dual_cols = jnp.einsum(
        "jab,jbc->jac", left_dual, summed, preferred_element_type=jnp.float32
    ).astype(jnp.bfloat16)
    dual_rows = lax.all_to_all(dual_cols, "sub", split_axis=1, concat_axis=2, tiled=True)
    mixed = jnp.einsum("jrn,jmn->jrm", dual_rows, right_dual, preferred_element_type=jnp.float32)
    scaled = (mixed / (left_rates[:, :, None] + right_rates[:, None, :])).astype(jnp.bfloat16)
    basis_rows = jnp.einsum(
        "jrm,jkm->jrk", scaled, right_eigenvector_matrix, preferred_element_type=jnp.float32
    ).astype(jnp.bfloat16)
    basis_cols = lax.all_to_all(basis_rows, "sub", split_axis=2, concat_axis=1, tiled=True)
    return jnp.einsum("jab,jbc->jac", left_basis, basis_cols, preferred_element_type=jnp.float32)


def solution(mesh):
    placed = (
        P("blk", "sub", None),
        P(),
        P(),
        P(),
        P(),
        P("blk", None, None),
        P("blk", None, None),
        P("blk", None, None),
        P("blk", None, None),
        P("blk", "sub"),
        P("blk", None),
    )
    return jax.shard_map(
        local, mesh=mesh, in_specs=placed, out_specs=P("blk", None, "sub"), check_vma=False
    )
```

profile of v0, /device:TPU:24, one launch (start us, length us, event | category | flops | bytes accessed | tf_op | source)
XLA Modules:
  0.0 166.9 jit_solution(14784271772205998171)
XLA Ops:
  6.5 0.0 copy-start
  6.5 0.0 all-gather.2.cloned.1.call-start
  6.5 0.7 all-gather.2.cloned.1.call-update
  7.3 1.1 constant_dynamic-slice_fusion
  8.3 0.1 copy.25
  8.4 0.9 dynamic-slice_reduce_fusion
  9.4 54.0 %all-gather.2.cloned.1.call-done = bf16[64,64,512]{2,1,0:T(8,128)(2,1)} async-done(((bf16[2,64,512]{2,1,0:T(8,128)(2,1)}), bf16[64,64,512]{2,1,0:T(8,128)(2,1)}) %all-gather.2.cloned.1.call-update) | async-done | bytes 4194320 | tf_op jit(solution)/shard_map/all_gather | solution.py:38
  63.4 6.7 %fusion.15 = bf16[2,8,64,512]{3,1,0,2:T(8,128)(2,1)S(1)} fusion(bf16[64,64,512]{2,1,0:T(8,128)(2,1)} %all-gather.2.cloned.1.call-done, s32[32,2]{0,1:T(2,128)S(1)} %get-tuple-element.6, bf16[32,2]{0,1:T(2,128)(2,1)S(1)} %compare_convert_fusion, s32[32,2]{0,1:T(2,128)S(1)} %get-tuple-element.5), kind=kOutput, calls=%fused_computation.10 | convolution fusion | flops 67770368 | bytes 5243520 | tf_op jit(solution)/shard_map/ks,srn->krn/dot_general | solution.py:39
  70.1 4.8 %fusion.12 = bf16[2,8,64,512]{3,2,0,1:T(8,128)(2,1)} fusion(bf16[8,512,512]{2,1,0:T(8,128)(2,1)} %param.13, bf16[2,8,64,512]{3,1,0,2:T(8,128)(2,1)S(1)} %fusion.15), kind=kOutput, calls=%fused_computation.9 | convolution fusion | flops 537395200 | bytes 6291456 | tf_op jit(solution)/shard_map/ktrn,tmn->ktrm/dot_general | solution.py:43
  74.9 4.7 %copy.28 = bf16[2,8,64,512]{2,0,1,3:T(2,128)(2,1)S(1)} copy(bf16[2,8,64,512]{3,2,0,1:T(8,128)(2,1)} %fusion.12) | data formatting | bytes 2097152 | tf_op jit(solution)/shard_map/convert_element_type | solution.py:45
  79.7 2.7 %reshape.46 = bf16[8,2,32768]{2,1,0:T(2,128)(2,1)} reshape(bf16[512,8,2,64]{3,2,1,0:T(2,128)(2,1)S(1)} %bitcast.85) | data formatting | bytes 2097152
  82.3 36.3 %all_to_all.54 = bf16[8,2,32768]{2,1,0:T(2,128)(2,1)} all-to-all(bf16[8,2,32768]{2,1,0:T(2,128)(2,1)} %reshape.46), channel_id=1, replica_groups=mesh['blk'=32,'sub'=8] {'sub'}, dimensions={0} | all-to-all | bytes 2097152 | tf_op jit(solution)/shard_map/all_to_all | solution.py:46
  118.6 3.1 %reshape.47 = bf16[512,8,2,64]{3,2,1,0:T(2,128)(2,1)S(1)} reshape(bf16[8,2,32768]{2,1,0:T(2,128)(2,1)} %all_to_all.54) | data formatting | bytes 2097152
  121.7 2.7 %copy.47 = bf16[2,8,64,8,64]{2,3,4,1,0:T(8,128)(2,1)} copy(bf16[2,8,64,8,64]{2,0,1,4,3:T(2,128)(2,1)S(1)} %bitcast.86) | data formatting | bytes 2097152 | tf_op jit(solution)/shard_map/all_to_all | solution.py:46
  124.4 3.2 %all_to_all.42 = bf16[2,8,512,64]{2,3,1,0:T(8,128)(2,1)S(1)} reshape(bf16[2,8,8,64,64]{3,2,4,1,0:T(8,128)(2,1)} %bitcast.87) | data formatting | bytes 2097152 | tf_op jit(solution)/shard_map/all_to_all | solution.py:46
  127.6 0.0 copy-done
  127.6 0.0 copy-start.2
  127.6 0.0 copy-start.3
  127.6 4.0 %fusion.25 = bf16[2,512,64]{1,2,0:T(8,128)(2,1)S(1)} fusion(bf16[2,512,512]{2,1,0:T(8,128)(2,1)S(1)} %copy-done, bf16[2,8,512,64]{2,3,1,0:T(8,128)(2,1)S(1)} %all_to_all.42, bf16[8,512,512]{2,1,0:T(8,128)(2,1)} %param.12), kind=kOutput, calls=%fused_computation.18 | convolution fusion | flops 604110848 | bytes 6422528 | tf_op jit(solution)/shard_map/jab,jbc->jac/dot_general | solution.py:50
  131.6 0.0 copy-start.1
  131.6 0.2 copy.30
  131.8 0.2 reshape.48
  132.0 11.5 %all_to_all.55 = bf16[8,2,4096]{2,1,0:T(2,128)(2,1)S(1)} all-to-all(bf16[8,2,4096]{2,1,0:T(2,128)(2,1)S(1)} %reshape.48), channel_id=1, replica_groups=mesh['blk'=32,'sub'=8] {'sub'}, dimensions={0} | all-to-all | bytes 262144 | tf_op jit(solution)/shard_map/all_to_all | solution.py:53
  143.5 0.2 reshape.49
  143.7 0.2 copy.49
  143.9 0.2 all_to_all.46
  144.1 0.0 copy-done.2
  144.1 0.0 copy-done.3
  144.1 2.3 %convolution_convert_fusion = bf16[2,64,512]{2,1,0:T(8,128)(2,1)S(1)} fusion(bf16[2,512,512]{2,1,0:T(8,128)(2,1)} %param.18, bf16[2,64,512]{2,1,0:T(8,128)(2,1)S(1)} %all_to_all.46, bf16[2,512,512]{2,1,0:T(8,128)(2,1)} %param.19, f32[2,512]{1,0:T(2,128)S(1)} %copy-done.2, f32[2,64]{1,0:T(2,128)S(1)} %copy-done.3), kind=kOutput, calls=%fused_computation.15 | convolution fusion | flops 134479872 | bytes 2363904 | tf_op jit(solution)/shard_map/jrm,jkm->jrk/dot_general | solution.py:56
  146.4 0.2 copy.32
  146.6 0.2 reshape.50
  146.8 11.5 %all_to_all.56 = bf16[8,2,4096]{2,1,0:T(2,128)(2,1)S(1)} all-to-all(bf16[8,2,4096]{2,1,0:T(2,128)(2,1)S(1)} %reshape.50), channel_id=1, replica_groups=mesh['blk'=32,'sub'=8] {'sub'}, dimensions={0} | all-to-all | bytes 262144 | tf_op jit(solution)/shard_map/all_to_all | solution.py:59
  158.3 0.2 reshape.51
  158.5 0.2 copy.48
  158.7 0.2 all_to_all.50
  158.9 0.0 copy-done.1
  158.9 1.1 convolution_bitcast_fusion
  (3 shorter events, 0.0 us)
Async XLA Ops:
  6.5 121.0 %copy-start = (bf16[2,512,512]{2,1,0:T(8,128)(2,1)S(1)}, bf16[2,512,512]{2,1,0:T(8,128)(2,1)}, u32[]{:S(2)}) copy-start(bf16[2,512,512]{2,1,0:T(8,128)(2,1)} %param.17) | copy-start | bytes 3145732
  6.5 56.8 %all-gather.2.cloned.1.call-start = ((), (), s32[]{:S(2)}) async-start(), calls=%async_computation.3 | async-start | bytes 4325376 | tf_op jit(solution)/shard_map/all_gather | solution.py:38
  127.6 16.5 %copy-start.2 = (f32[2,512]{1,0:T(2,128)S(1)}, f32[2,512]{1,0:T(2,128)}, u32[]{:S(2)}) copy-start(f32[2,512]{1,0:T(2,128)} %param.21) | copy-start | bytes 12292
  127.6 16.5 %copy-start.3 = (f32[2,64]{1,0:T(2,128)S(1)}, f32[2,64]{1,0:T(2,128)}, u32[]{:S(2)}) copy-start(f32[2,64]{1,0:T(2,128)} %param.20) | copy-start | bytes 1540
  131.6 27.3 %copy-start.1 = (bf16[2,512,512]{2,1,0:T(8,128)(2,1)S(1)}, bf16[2,512,512]{2,1,0:T(8,128)(2,1)}, u32[]{:S(2)}) copy-start(bf16[2,512,512]{2,1,0:T(8,128)(2,1)} %param.16) | copy-start | bytes 3145732
Sparse Core Ops, SparseCore 0:
  9.9 53.3 all-gather.1
where the time goes:
time: 168 us; the launch traced here: 167 us
  blocking collectives  59.2 us (35%)
  waiting for transfers between devices  54.7 us (33%)
  local copies, waits for them, and re-layouts  20.5 us (12%)
  matrix products  19 us (11%)
  between operations  13.6 us (8%)
    all_gather x1, waiting for transfers between devices, local(): everything = lax.all_gather(block_vec, 'blk', axis=0, tiled=True)  54 us
    all_to_all x1, blocking collectives, local(): lax.all_to_all(right_done, 'sub', split_axis=3, concat_axis=2, tiled=True)  36.3 us
    all_to_all x1, blocking collectives, local(): lax.all_to_all(dual_cols, 'sub', split_axis=1, concat_axis=2, tiled=True)  11.5 us
    all_to_all x1, blocking collectives, local(): lax.all_to_all(basis_rows, 'sub', split_axis=2, concat_axis=1, tiled=True)  11.5 us
    dot_general x1, matrix products, local(): jnp.einsum('ks,srn->krn', weights, everything, preferred_element_type=jnp...  6.75 us
    unnamed x14, local copies, waits for them, and re-layouts  6.67 us
    all_to_all x2, local copies, waits for them, and re-layouts, local(): lax.all_to_all(right_done, 'sub', split_axis=3, concat_axis=2, tiled=True)  5.88 us
    dot_general x1, matrix products, local(): jnp.einsum('ktrn,tmn->ktrm', pooled, right_factor, preferred_element_type...  4.8 us
  transfers between devices with their start and end apart: 1, of which 1 were waited for; matrix products, arithmetic and copies ran while one was open for 1% of the time, Pallas kernels for 0%

commit v1 on v0

--- a/solution.py
+++ b/solution.py
@@ -18,6 +18,7 @@
     right_rates,
 ):
     owner = lax.axis_index("blk")
+    part = lax.axis_index("sub")
     groups = lax.axis_size("blk")
     local_blocks = block_vec.shape[0]
     row_count = block_vec.shape[1]
@@ -25,6 +26,7 @@
     slots_per = pairs.shape[2]
     term_total = left_factor.shape[0]
     all_count = groups * local_blocks
+    next_cols = width_two // lax.axis_size("sub")
     incoming = lax.dynamic_index_in_dim(pairs, owner, 1, keepdims=False)
     counts = lax.dynamic_index_in_dim(pair_count, owner, 1, keepdims=False)
     live_mask = (jnp.arange(slots_per)[None, :] < counts[:, None]).astype(jnp.float32)
@@ -35,6 +37,7 @@
     ).astype(jnp.float32) * live_mask[..., None]
     source_onehot = (source[..., None] == jnp.arange(all_count)[None, None, :]).astype(jnp.float32)
     weights = jnp.einsum("gqk,gqs->ks", key_onehot, source_onehot).astype(jnp.bfloat16)
+    rates_full = lax.all_gather(left_rates, "sub", axis=1, tiled=True)
     everything = lax.all_gather(block_vec, "blk", axis=0, tiled=True)
     pooled = jnp.einsum(
         "ks,srn->krn", weights, everything, preferred_element_type=jnp.float32
@@ -43,20 +46,20 @@
     right_done = jnp.einsum(
         "ktrn,tmn->ktrm", pooled, right_factor, preferred_element_type=jnp.float32
     ).astype(jnp.bfloat16)
-    right_cols = lax.all_to_all(right_done, "sub", split_axis=3, concat_axis=2, tiled=True)
-    summed = jnp.einsum(
-        "tab,ktbc->kac", left_factor, right_cols, preferred_element_type=jnp.float32
+    left_part = lax.dynamic_slice_in_dim(left_factor, part * row_count, row_count, axis=2)
+    partial = jnp.einsum(
+        "tab,ktbc->kac", left_part, right_done, preferred_element_type=jnp.float32
     ).astype(jnp.bfloat16)
+    summed = lax.psum(partial, "sub")
     dual_cols = jnp.einsum(
         "jab,jbc->jac", left_dual, summed, preferred_element_type=jnp.float32
     ).astype(jnp.bfloat16)
-    dual_rows = lax.all_to_all(dual_cols, "sub", split_axis=1, concat_axis=2, tiled=True)
-    mixed = jnp.einsum("jrn,jmn->jrm", dual_rows, right_dual, preferred_element_type=jnp.float32)
-    scaled = (mixed / (left_rates[:, :, None] + right_rates[:, None, :])).astype(jnp.bfloat16)
-    basis_rows = jnp.einsum(
-        "jrm,jkm->jrk", scaled, right_eigenvector_matrix, preferred_element_type=jnp.float32
+    mixed = jnp.einsum("jrn,jmn->jrm", dual_cols, right_dual, preferred_element_type=jnp.float32)
+    scaled = (mixed / (rates_full[:, :, None] + right_rates[:, None, :])).astype(jnp.bfloat16)
+    eig_part = lax.dynamic_slice_in_dim(right_eigenvector_matrix, part * next_cols, next_cols, axis=1)
+    basis_cols = jnp.einsum(
+        "jrm,jkm->jrk", scaled, eig_part, preferred_element_type=jnp.float32
     ).astype(jnp.bfloat16)
-    basis_cols = lax.all_to_all(basis_rows, "sub", split_axis=2, concat_axis=1, tiled=True)
     return jnp.einsum("jab,jbc->jac", left_basis, basis_cols, preferred_element_type=jnp.float32)
 
 

time: 168 us -> 167 us (level)
  waiting for transfers between devices: 54.7 us -> 114 us
  blocking collectives: 59.2 us -> 16.7 us
  local copies, waits for them, and re-layouts: 20.5 us -> 2.19 us
    all_to_all x3 -> x0, blocking collectives: 59.2 us -> none  [the longest x1 36.3 us: local(): lax.all_to_all(right_done, 'sub', split_axis=3, concat_axis=2, tiled=True)]
    psum x0 -> x1, waiting for transfers between devices: none -> 59 us  [local(): summed = lax.psum(partial, 'sub')]
    all_gather x0 -> x1, blocking collectives: none -> 16.7 us  [local(): rates_full = lax.all_gather(left_rates, 'sub', axis=1, tiled=True)]
    all_to_all x6 -> x0, local copies, waits for them, and re-layouts: 6.65 us -> none  [the longest x2 5.88 us: local(): lax.all_to_all(right_done, 'sub', split_axis=3, concat_axis=2, tiled=True)]
    unnamed x14 -> x11, local copies, waits for them, and re-layouts: 6.67 us -> 0.1 us
    convert_element_type x3 -> x0, local copies, waits for them, and re-layouts: 5.07 us -> none  [the longest x1 4.74 us: local(): right_done = jnp.einsum('ktrn,tmn->ktrm', pooled, right_factor, preferred...]
    dot_general x2, matrix products: 7.1 us -> 9.25 us  [the longest x1 6.76 us: local(): jnp.einsum('tab,ktbc->kac', left_part, right_done, preferred_element_type...]
  transfers between devices with their start and end apart: 1 -> 2, of which waited for: 1 -> 2; matrix products, arithmetic and copies ran while one was open for 1% -> 1% of each run, Pallas kernels for 0% -> 0%
where the time goes in v1:
time: 167 us; the launch traced here: 166 us
  waiting for transfers between devices  114 us (68%)
  matrix products  20.1 us (12%)
  blocking collectives  16.7 us (10%)
  between operations  13.5 us (8%)
  local copies, waits for them, and re-layouts  2.19 us (1%)
    psum x1, waiting for transfers between devices, local(): summed = lax.psum(partial, 'sub')  59 us
    all_gather x1, waiting for transfers between devices, local(): everything = lax.all_gather(block_vec, 'blk', axis=0, tiled=True)  53.9 us
    all_gather x1, blocking collectives, local(): rates_full = lax.all_gather(left_rates, 'sub', axis=1, tiled=True)  16.7 us
    dot_general x1, matrix products, local(): jnp.einsum('tab,ktbc->kac', left_part, right_done, preferred_element_type...  6.76 us
    dot_general x1, matrix products, local(): jnp.einsum('ks,srn->krn', weights, everything, preferred_element_type=jnp...  6.75 us
  transfers between devices with their start and end apart: 2, of which 2 were waited for; matrix products, arithmetic and copies ran while one was open for 1% of the time, Pallas kernels for 0%

profile of v1, /device:TPU:24, one launch (start us, length us, event | category | flops | bytes accessed | tf_op | source)
XLA Modules:
  0.0 166.3 jit_solution(6176274853760722163)
XLA Ops:
  6.5 0.0 copy-start
  6.5 0.0 all-gather.3.cloned.1.call-start
  6.5 0.7 all-gather.3.cloned.1.call-update
  7.3 0.0 all-reduce.2.cloned.1.call-start
  7.3 1.1 constant_dynamic-slice_fusion
  8.4 0.1 copy.20
  8.5 0.9 dynamic-slice_reduce_fusion
  9.4 53.9 %all-gather.3.cloned.1.call-done = bf16[64,64,512]{2,1,0:T(8,128)(2,1)} async-done(((bf16[2,64,512]{2,1,0:T(8,128)(2,1)}), bf16[64,64,512]{2,1,0:T(8,128)(2,1)}) %all-gather.3.cloned.1.call-update) | async-done | bytes 4194320 | tf_op jit(solution)/shard_map/all_gather | solution.py:41
  63.4 6.7 %fusion.13 = bf16[2,8,64,512]{3,1,0,2:T(8,128)(2,1)S(1)} fusion(bf16[64,64,512]{2,1,0:T(8,128)(2,1)} %all-gather.3.cloned.1.call-done, s32[32,2]{0,1:T(2,128)S(1)} %get-tuple-element.6, bf16[32,2]{0,1:T(2,128)(2,1)S(1)} %compare_convert_fusion, s32[32,2]{0,1:T(2,128)S(1)} %get-tuple-element.5), kind=kOutput, calls=%fused_computation.10 | convolution fusion | flops 67770368 | bytes 5243520 | tf_op jit(solution)/shard_map/ks,srn->krn/dot_general | solution.py:42
  70.1 0.0 copy-start.2
  70.1 6.8 %fusion.16 = bf16[2,512,512]{1,2,0:T(8,128)(2,1)} fusion(bf16[8,512,512]{2,1,0:T(8,128)(2,1)} %param.12, s32[]{:T(128)S(6)} %select_n.11, bf16[8,512,512]{2,1,0:T(8,128)(2,1)} %param.13, bf16[2,8,64,512]{3,1,0,2:T(8,128)(2,1)S(1)} %fusion.13), kind=kOutput, calls=%fused_computation.11 | convolution fusion | flops 1074790400 | bytes 7340036 | tf_op jit(solution)/shard_map/tab,ktbc->kac/dot_general | solution.py:50
  76.9 0.0 copy-start.3
  76.9 0.0 copy-start.4
  76.9 0.0 all-reduce.2.cloned.1.call-update
  76.9 0.0 copy-done.2
  76.9 16.7 %all-gather = f32[8,64,2]{1,2,0:T(2,128)S(1)} all-gather(f32[1,64,2]{1,2,0:T(2,128)S(1)} %bitcast.62), channel_id=1, replica_groups=mesh['blk'=32,'sub'=8] {'sub'}, dimensions={0}, use_global_device_ids=true | all-gather | bytes 4608 | tf_op jit(solution)/shard_map/all_gather | solution.py:40
  93.6 0.1 reshape.41
  93.7 59.0 %all-reduce.2.cloned.1.call-done = bf16[2,512,512]{1,2,0:T(8,128)(2,1)} async-done(((bf16[2,512,512]{1,2,0:T(8,128)(2,1)}), bf16[2,512,512]{1,2,0:T(8,128)(2,1)}) %all-reduce.2.cloned.1.call-update) | async-done | bytes 1048592 | tf_op jit(solution)/shard_map/psum | solution.py:53
  152.8 0.0 copy-done
  152.8 3.0 %convolution_convert_fusion = bf16[2,512,512]{2,1,0:T(8,128)(2,1)} fusion(bf16[2,512,512]{1,2,0:T(8,128)(2,1)} %all-reduce.2.cloned.1.call-done, bf16[2,512,512]{2,1,0:T(8,128)(2,1)S(1)} %copy-done), kind=kOutput, calls=%fused_computation.8 | convolution fusion | flops 537395200 | bytes 3145728 | tf_op jit(solution)/shard_map/jab,jbc->jac/dot_general | solution.py:54
  155.8 0.0 copy-done.3
  155.8 0.0 copy-done.4
  155.8 0.0 copy-start.1
  155.8 2.5 %fusion.18 = bf16[2,512,64]{1,2,0:T(8,128)(2,1)S(1)} fusion(bf16[2,512,512]{2,1,0:T(8,128)(2,1)} %convolution_convert_fusion, bf16[2,512,512]{2,1,0:T(8,128)(2,1)S(1)} %copy-done.3, f32[2,512]{1,0:T(2,128)S(1)} %copy-done.4, f32[2,512]{1,0:T(2,128)S(1)} %bitcast.61, bf16[2,512,512]{2,1,0:T(8,128)(2,1)} %param.18, s32[]{:T(128)S(6)} %select_n.11), kind=kOutput, calls=%fused_computation.14 | convolution fusion | flops 605618176 | bytes 2367492 | tf_op jit(solution)/shard_map/jrm,jkm->jrk/dot_general | solution.py:60
  158.3 0.0 copy-done.1
  158.3 1.1 convolution_bitcast_fusion
  (4 shorter events, 0.0 us)
Async XLA Ops:
  6.5 146.2 %copy-start = (bf16[2,512,512]{2,1,0:T(8,128)(2,1)S(1)}, bf16[2,512,512]{2,1,0:T(8,128)(2,1)}, u32[]{:S(2)}) copy-start(bf16[2,512,512]{2,1,0:T(8,128)(2,1)} %param.17) | copy-start | bytes 3145732
  6.5 56.8 %all-gather.3.cloned.1.call-start = ((), (), s32[]{:S(2)}) async-start(), calls=%async_computation | async-start | bytes 4325376 | tf_op jit(solution)/shard_map/all_gather | solution.py:41
  7.3 145.5 %all-reduce.2.cloned.1.call-start = ((), (), s32[]{:S(2)}) async-start(), calls=%async_computation.1 | async-start | bytes 2097152 | tf_op jit(solution)/shard_map/psum | solution.py:53
  70.1 6.8 %copy-start.2 = (f32[2,64]{1,0:T(2,128)S(1)}, f32[2,64]{1,0:T(2,128)}, u32[]{:S(2)}) copy-start(f32[2,64]{1,0:T(2,128)} %param.20) | copy-start | bytes 1540
  76.9 78.9 %copy-start.3 = (bf16[2,512,512]{2,1,0:T(8,128)(2,1)S(1)}, bf16[2,512,512]{2,1,0:T(8,128)(2,1)}, u32[]{:S(2)}) copy-start(bf16[2,512,512]{2,1,0:T(8,128)(2,1)} %param.19) | copy-start | bytes 3145732
  76.9 78.9 %copy-start.4 = (f32[2,512]{1,0:T(2,128)S(1)}, f32[2,512]{1,0:T(2,128)}, u32[]{:S(2)}) copy-start(f32[2,512]{1,0:T(2,128)} %param.21) | copy-start | bytes 12292
  155.8 2.5 %copy-start.1 = (bf16[2,512,512]{2,1,0:T(8,128)(2,1)S(1)}, bf16[2,512,512]{2,1,0:T(8,128)(2,1)}, u32[]{:S(2)}) copy-start(bf16[2,512,512]{2,1,0:T(8,128)(2,1)} %param.16) | copy-start | bytes 3145732
Sparse Core Ops, SparseCore 0:
  9.9 53.3 all-gather.2
  77.0 75.7 all-reduce.1
